TPU v7x, 256 devices: a whole 4x4x8 slice. The times are simulated.
256 devices in a mesh: dp: 32 (over z, x), et: 8 (over y, core).
Axes of the slice: x: 4, y: 4, z: 8, core: 2. Of those that a mesh axis runs over, the one named last changes fastest.
Arguments:
- tokens: bfloat16 [4096, 2048], P('dp', 'et'), may hold values from -6 to 6
- cotangent: bfloat16 [4096, 2048], P('dp', 'et'), may hold values from -1.5 to 1.5
- expert_ids: int32 [4096, 8], P('dp'), may hold values from 0 to 63, all different within a row; in each aligned block of 128 rows (0 to 127, 128 to 255, ...) at most 24 rows name the same one
- route_gates: bfloat16 [4096, 8], P('dp'), may hold values from 0.049804688 to 0.3984375
- gate_proj: bfloat16 [64, 2048, 1024], P('dp', None, 'et'), may hold values from -0.125 to 0.125
- up_proj: bfloat16 [64, 2048, 1024], P('dp', None, 'et'), may hold values from -0.125 to 0.125
- down_proj: bfloat16 [64, 1024, 2048], P('dp', 'et'), may hold values from -0.1875 to 0.1875
Outputs:
- mixed: bfloat16 [4096, 2048], P('dp', 'et')
- grad_tokens: bfloat16 [4096, 2048], P('dp', 'et')
- grad_gates: float32 [4096, 8], P('dp')
- grad_gate_proj: float32 [64, 2048, 1024], P('dp', None, 'et')
- grad_up_proj: float32 [64, 2048, 1024], P('dp', None, 'et')
- grad_down_proj: float32 [64, 1024, 2048], P('dp', 'et')
Inputs may be any that keep to these rules, and one draw needn't show every extreme that they name: `expert_ids`: each row names 8 different experts. Among the rows of one device (128 aligned rows), no expert is named more than 24 times, a bound that some block reaches.
All inputs are finite; a program needn't handle non-finite values.
Results may differ from a plain program's by a relative error of at most 0.015.
Values may be sent and summed in bfloat16 or wider, within the bound.
No kernel may reach another device: no remote copies, remote signals or barrier semaphores. Data moves between devices by JAX's collectives and lax.ppermute only.
A program may use at most 128 MiB of HBM per device.

v0:
```python
import jax
import jax.numpy as jnp
from jax import lax
from jax.sharding import PartitionSpec as P


def places_in_block(chosen, experts):
    flattened = chosen.reshape(-1)
    pairs = flattened.shape[0]
    onehot = (flattened[:, None] == jnp.arange(experts, dtype=jnp.int32)[None, :]).astype(
        jnp.bfloat16
    )
    rows = lax.broadcasted_iota(jnp.int32, (pairs, pairs), 0)
    cols = lax.broadcasted_iota(jnp.int32, (pairs, pairs), 1)
    earlier = (cols < rows).astype(jnp.bfloat16)
    before = jnp.dot(earlier, onehot, preferred_element_type=jnp.float32)
    return jnp.sum(before * onehot.astype(jnp.float32), axis=1).astype(jnp.int32)


def local(tokens, cotangent, expert_ids, route_gates, gate_proj, up_proj, down_proj):
    groups = lax.axis_size("dp")
    shards = lax.axis_size("et")
    local_experts, features, units = gate_proj.shape
    experts = local_experts * groups
    tok_rows, per_token = expert_ids.shape
    width = tokens.shape[1]
    capacity = 3 * tok_rows * per_token // (2 * experts)
    slots = experts * capacity
    places = places_in_block(expert_ids, experts)
    slot_index = (expert_ids.reshape(-1) * capacity + places).reshape(tok_rows, per_token)
    by_pair = slot_index.T
    match = by_pair[None, :, :] == jnp.arange(slots, dtype=jnp.int32)[:, None, None]
    select = jnp.any(match, axis=1).astype(jnp.bfloat16)
    gate_select = jnp.sum(
        jnp.where(match, route_gates.T[None, :, :].astype(jnp.float32), 0.0), axis=1
    ).astype(jnp.bfloat16)
    picked = jnp.dot(select, tokens, preferred_element_type=jnp.float32).astype(jnp.bfloat16)
    scaled = jnp.dot(gate_select, cotangent, preferred_element_type=jnp.float32).astype(
        jnp.bfloat16
    )
    routed = jnp.stack([picked, scaled]).reshape(2, experts, capacity, width)
    routed = lax.all_to_all(routed, "dp", split_axis=1, concat_axis=2, tiled=True)
    gathered = lax.all_gather(routed, "et", axis=0)
    expert_in = gathered[:, 0]
    expert_cot = gathered[:, 1]
    gate_w = gate_proj.reshape(local_experts, shards, width, units)
    up_w = up_proj.reshape(local_experts, shards, width, units)
    down_w = down_proj.reshape(local_experts, units, shards, width)
    pre_gate = jnp.einsum("jesd,ejdf->esf", expert_in, gate_w, preferred_element_type=jnp.float32)
    pre_up = jnp.einsum("jesd,ejdf->esf", expert_in, up_w, preferred_element_type=jnp.float32)
    sigmoid_gate = jax.nn.sigmoid(pre_gate)
    silu_gate = pre_gate * sigmoid_gate
    hidden = (silu_gate * pre_up).astype(jnp.bfloat16)
    out_part = jnp.einsum("esf,efd->esd", hidden, down_proj, preferred_element_type=jnp.float32)
    grad_hidden = jnp.einsum(
        "jesd,efjd->esf", expert_cot, down_w, preferred_element_type=jnp.float32
    )
    grad_pre_gate = (
        grad_hidden * pre_up * sigmoid_gate * (1.0 + pre_gate * (1.0 - sigmoid_gate))
    ).astype(jnp.bfloat16)
    grad_pre_up = (grad_hidden * silu_gate).astype(jnp.bfloat16)
    grad_down = jnp.einsum(
        "esf,jesd->efjd", hidden, expert_cot, preferred_element_type=jnp.float32
    ).reshape(local_experts, units, features)
    grad_gate_w = jnp.einsum(
        "jesd,esf->ejdf", expert_in, grad_pre_gate, preferred_element_type=jnp.float32
    ).reshape(local_experts, features, units)
    grad_up_w = jnp.einsum(
        "jesd,esf->ejdf", expert_in, grad_pre_up, preferred_element_type=jnp.float32
    ).reshape(local_experts, features, units)
    in_part = jnp.einsum(
        "esf,edf->esd", grad_pre_gate, gate_proj, preferred_element_type=jnp.float32
    )
    in_part = in_part + jnp.einsum(
        "esf,edf->esd", grad_pre_up, up_proj, preferred_element_type=jnp.float32
    )
    out_sum, in_sum = (
        lax.psum_scatter(out_part.astype(jnp.bfloat16), "et", scatter_dimension=2, tiled=True),
        lax.psum_scatter(in_part.astype(jnp.bfloat16), "et", scatter_dimension=2, tiled=True),
    )
    back_out, back_grad = (
        lax.all_to_all(out_sum, "dp", split_axis=1, concat_axis=0, tiled=True),
        lax.all_to_all(in_sum, "dp", split_axis=1, concat_axis=0, tiled=True),
    )
    back_out = back_out.reshape(slots, width)
    back_grad = back_grad.reshape(slots, width)
    mixed = jnp.einsum(
        "st,sd->td", gate_select, back_out, preferred_element_type=jnp.float32
    ).astype(jnp.bfloat16)
    grad_tokens = jnp.einsum(
        "st,sd->td", select, back_grad, preferred_element_type=jnp.float32
    ).astype(jnp.bfloat16)
    out_rows = (
        back_out[slot_index.reshape(-1)].reshape(tok_rows, per_token, width).astype(jnp.float32)
    )
    gate_part = jnp.sum(cotangent.astype(jnp.float32)[:, None, :] * out_rows, axis=2)
    grad_gates = lax.psum(gate_part, "et")
    return (mixed, grad_tokens, grad_gates, grad_gate_w, grad_up_w, grad_down)


def solution(mesh):
    in_specs = (
        P("dp", "et"),
        P("dp", "et"),
        P("dp", None),
        P("dp", None),
        P("dp", None, "et"),
        P("dp", None, "et"),
        P("dp", "et", None),
    )
    out_specs = (
        P("dp", "et"),
        P("dp", "et"),
        P("dp", None),
        P("dp", None, "et"),
        P("dp", None, "et"),
        P("dp", "et", None),
    )
    return jax.shard_map(local, mesh=mesh, in_specs=in_specs, out_specs=out_specs, check_vma=False)
```

profile of v0, /device:TPU:2, one launch (start us, length us, event | category | flops | bytes accessed | tf_op | source)
XLA Modules:
  0.0 328.7 jit_solution(484087539045145669)
XLA Ops:
  7.2 0.0 copy-start
  7.2 0.0 all-gather.2.cloned.1.call-start
  7.2 0.8 convert_bitcast_fusion
  8.0 0.8 copy.65
  8.8 0.1 eq.28
  8.9 0.6 fusion.12
  9.5 0.1 convert_element_type.78
  9.6 5.6 %fusion = pred[1536,128]{1,0:T(8,128)(4,1)S(1)} fusion(s32[8,128]{1,0:T(8,128)S(1)} %copy.67), kind=kLoop, calls=%fused_computation.6 | loop fusion | flops 2949120 | bytes 200704 | tf_op jit(solution)/shard_map/reduce_or | solution.py:33
  15.2 0.0 copy-start.11
  15.2 8.1 %select_reduce_fusion = bf16[1536,128]{1,0:T(8,128)(2,1)S(1)} fusion(f32[8,128]{1,0:T(8,128)S(1)} %convert_bitcast_fusion, s32[8,128]{1,0:T(8,128)S(1)} %copy.67), kind=kLoop, calls=%fused_computation.4 | loop fusion | flops 4521984 | bytes 401408 | tf_op jit(solution)/shard_map/reduce_sum | solution.py:34
  23.4 1.2 convolution_convert_fusion.1
  24.6 0.0 copy-start.9
  24.6 1.3 convolution_convert_fusion.2
  25.9 0.0 copy-done.11
  25.9 0.1 pad_maximum_fusion
  26.1 50.7 %all_to_all.45 = bf16[2,64,24,256]{3,2,0,1:T(8,128)(2,1)S(1)} all-to-all(bf16[2,64,24,256]{3,2,0,1:T(8,128)(2,1)S(1)} %pad_maximum_fusion), channel_id=1, replica_groups=mesh['dp'=32,'et'=8] {'dp'}, dimensions={1} | all-to-all | bytes 3145728 | tf_op jit(solution)/shard_map/all_to_all | solution.py:42
  76.8 1.2 copy.70
  78.0 0.0 all-gather.2.cloned.1.call-update
  78.0 0.2 reduce-scatter.3.cloned.1.call-start
  78.3 66.7 %all-gather.2.cloned.1.call-done = bf16[8,2,2,768,256]{4,3,0,2,1:T(8,128)(2,1)} async-done(((bf16[1,2,2,768,256]{4,3,0,2,1:T(8,128)(2,1)}), bf16[8,2,2,768,256]{4,3,0,2,1:T(8,128)(2,1)}) %all-gather.2.cloned.1.call-update) | async-done | bytes 12582928 | tf_op jit(solution)/shard_map/all_gather | solution.py:43
  144.9 0.0 copy-done.9
  145.0 4.7 %fusion.9 = f32[2,768,128]{2,1,0:T(8,128)S(1)} fusion(bf16[2,8,256,128]{3,2,1,0:T(8,128)(2,1)S(1)} %bitcast.108, bf16[8,2,2,768,256]{4,3,0,2,1:T(8,128)(2,1)} %all-gather.2.cloned.1.call-done), kind=kOutput, calls=%fused_computation.20 | convolution fusion | flops 805306368 | bytes 8126464 | tf_op jit(solution)/shard_map/jesd,ejdf->esf/dot_general | solution.py:50
  149.7 0.0 copy-done
  149.7 0.0 copy-start.10
  149.7 5.2 %fusion.8 = f32[2,768,128]{2,1,0:T(8,128)S(1)} fusion(bf16[2,8,256,128]{3,2,1,0:T(8,128)(2,1)S(1)} %bitcast.96, bf16[8,2,2,768,256]{4,3,0,2,1:T(8,128)(2,1)} %all-gather.2.cloned.1.call-done), kind=kOutput, calls=%fused_computation.19 | convolution fusion | flops 805306368 | bytes 8126464 | tf_op jit(solution)/shard_map/jesd,ejdf->esf/dot_general | solution.py:49
  154.9 0.0 copy-done.2
  154.9 0.0 copy-done.10
  154.9 2.0 multiply_convert_fusion
  156.9 0.0 copy-start.8
  157.0 0.0 copy-start.5
  157.0 0.0 copy-start.7
  157.0 0.7 copy-done.8
  157.7 4.4 %convolution_convert_fusion = bf16[2,768,2048]{2,1,0:T(8,128)(2,1)} fusion(bf16[2,768,128]{2,1,0:T(8,128)(2,1)S(1)} %get-tuple-element.32, bf16[2,128,2048]{2,1,0:T(8,128)(2,1)S(1)} %copy-done.10), kind=kOutput, calls=%fused_computation.9 | convolution fusion | flops 808452096 | bytes 7733248 | tf_op jit(solution)/shard_map/esf,efd->esd/dot_general | solution.py:54
  162.1 0.0 reduce-scatter.3.cloned.1.call-update
  162.1 0.0 reduce-scatter.5.cloned.1.call-start
  162.2 0.0 copy-done.5
  162.2 1.8 fusion.24
  164.0 4.4 %add_convert_fusion = bf16[2,768,2048]{2,1,0:T(8,128)(2,1)} fusion(f32[2,768,2048]{2,1,0:T(8,128)S(1)} %fusion.24, bf16[2,768,128]{2,1,0:T(8,128)(2,1)S(1)} %get-tuple-element.30, bf16[2,2048,128]{2,1,0:T(8,128)(2,1)S(1)} %copy-done.9), kind=kOutput, calls=%fused_computation.1 | convolution fusion | flops 811597824 | bytes 20316160 | tf_op jit(solution)/shard_map/esf,edf->esd/dot_general | solution.py:74
  168.4 0.0 reduce-scatter.5.cloned.1.call-update
  168.4 39.3 %reduce-scatter.3.cloned.1.call-done = bf16[2,768,256]{2,1,0:T(8,128)(2,1)} async-done(((bf16[2,768,2048]{2,1,0:T(8,128)(2,1)}), bf16[2,768,256]{2,1,0:T(8,128)(2,1)}) %reduce-scatter.3.cloned.1.call-update) | async-done | bytes 786448 | tf_op jit(solution)/shard_map/reduce_scatter | solution.py:78
  207.7 2.8 copy.71
  210.5 10.1 %all-to-all-start.1 = ((bf16[2,768,256]{2,0,1:T(2,128)(2,1)}), bf16[2,768,256]{2,0,1:T(2,128)(2,1)S(1)}, u32[]{:S(2)}, u32[]{:S(2)}) async-start(bf16[2,768,256]{2,0,1:T(2,128)(2,1)} %copy.71), calls=%async_computation.2 | async-start | bytes 1572864 | tf_op jit(solution)/shard_map/all_to_all | solution.py:82
  220.7 0.0 copy-done.14
  220.7 0.7 convert_element_type.91
  221.3 0.1 mul.64
  221.5 33.8 %reduce-scatter.5.cloned.1.call-done = bf16[2,768,256]{2,1,0:T(8,128)(2,1)} async-done(((bf16[2,768,2048]{2,1,0:T(8,128)(2,1)}), bf16[2,768,256]{2,1,0:T(8,128)(2,1)}) %reduce-scatter.5.cloned.1.call-update) | async-done | bytes 786448 | tf_op jit(solution)/shard_map/reduce_scatter | solution.py:79
  255.3 2.9 copy.74
  258.2 0.0 all-to-all-done.1
  258.2 10.1 %all-to-all-start.2 = ((bf16[2,768,256]{2,0,1:T(2,128)(2,1)}), bf16[2,768,256]{2,0,1:T(2,128)(2,1)}, u32[]{:S(2)}, u32[]{:S(2)}) async-start(bf16[2,768,256]{2,0,1:T(2,128)(2,1)} %copy.74), calls=%async_computation.4 | async-start | bytes 1572864 | tf_op jit(solution)/shard_map/all_to_all | solution.py:83
  268.3 5.5 %fusion.1 = f32[2,128,8,256]{1,3,2,0:T(8,128)S(1)} fusion(bf16[8,2,2,768,256]{4,3,0,2,1:T(8,128)(2,1)} %all-gather.2.cloned.1.call-done, bf16[2,768,128]{2,1,0:T(8,128)(2,1)} %copy-done.8), kind=kOutput, calls=%fused_computation.7 | convolution fusion | flops 805306368 | bytes 8781824 | tf_op jit(solution)/shard_map/esf,jesd->efjd/dot_general | solution.py:62
  273.8 1.8 copy.82
  275.6 6.7 %fusion.4 = f32[2,8,256,128]{3,2,1,0:T(8,128)} fusion(bf16[8,2,2,768,256]{4,3,0,2,1:T(8,128)(2,1)} %all-gather.2.cloned.1.call-done, bf16[2,768,128]{2,1,0:T(8,128)(2,1)} %copy-done.7), kind=kOutput, calls=%fused_computation.12 | convolution fusion | flops 805306368 | bytes 8781824 | tf_op jit(solution)/shard_map/jesd,esf->ejdf/dot_general | solution.py:68
  282.3 6.7 %fusion.5 = f32[2,8,256,128]{3,2,1,0:T(8,128)} fusion(bf16[8,2,2,768,256]{4,3,0,2,1:T(8,128)(2,1)} %all-gather.2.cloned.1.call-done, bf16[2,768,128]{2,1,0:T(8,128)(2,1)S(1)} %copy-done.6), kind=kOutput, calls=%fused_computation.13 | convolution fusion | flops 805306368 | bytes 8781824 | tf_op jit(solution)/shard_map/jesd,esf->ejdf/dot_general | solution.py:65
  289.1 0.1 copy.72
  289.2 3.9 %gather_fusion = bf16[1024,256]{1,0:T(8,128)(2,1)S(1)} fusion(bf16[1536,256]{1,0:T(8,128)(2,1)S(1)} %bitcast.97, s32[1024]{0:T(1024)S(1)} %broadcast_clamp_fusion), kind=kCustom, calls=%fused_computation | custom fusion | bytes 1052672 | tf_op jit(solution)/shard_map/gather | solution.py:94
  293.2 0.2 fusion.15
  293.4 24.7 %psum.7 = f32[128,8]{1,0:T(8,128)S(1)} all-reduce(f32[128,8]{1,0:T(8,128)S(1)} %fusion.15), channel_id=1, replica_groups=mesh['dp'=32,'et'=8] {'et'}, use_global_device_ids=true, to_apply=%region_6.7 | all-reduce | flops 1024 | bytes 8192 | tf_op jit(solution)/shard_map/psum | solution.py:97
  318.1 0.7 copy.81
  318.8 1.0 convolution_convert_fusion.3
  319.7 0.0 all-to-all-done.2
  319.7 1.2 copy.75
  321.0 0.1 copy.76
  321.0 0.0 copy-done.12
  321.1 1.1 convolution_convert_fusion.4
  (19 shorter events, 0.1 us)
Async XLA Ops:
  7.2 142.5 %copy-start = (bf16[2,2048,128]{2,1,0:T(8,128)(2,1)S(1)}, bf16[2,2048,128]{2,1,0:T(8,128)(2,1)}, u32[]{:S(2)}) copy-start(bf16[2,2048,128]{2,1,0:T(8,128)(2,1)} %param.11) | copy-start | bytes 3145732
  7.2 137.8 %all-gather.2.cloned.1.call-start = ((), (), s32[]{:S(2)}) async-start(), calls=%async_computation.5 | async-start | bytes 14155776 | tf_op jit(solution)/shard_map/all_gather | solution.py:43
  15.2 10.7 %copy-start.11 = (pred[1536,128]{1,0:T(8,128)(4,1)}, pred[1536,128]{1,0:T(8,128)(4,1)S(1)}, u32[]{:S(2)}) copy-start(pred[1536,128]{1,0:T(8,128)(4,1)S(1)} %fusion) | copy-start | bytes 589828
  24.6 120.4 %copy-start.9 = (bf16[2,2048,128]{2,1,0:T(8,128)(2,1)S(1)}, bf16[2,2048,128]{2,1,0:T(8,128)(2,1)}, u32[]{:S(2)}) copy-start(bf16[2,2048,128]{2,1,0:T(8,128)(2,1)} %param.12) | copy-start | bytes 3145732
  78.0 129.7 %reduce-scatter.3.cloned.1.call-start = ((), (), s32[]{:S(2)}) async-start(), calls=%async_computation.6 | async-start | bytes 7077888 | tf_op jit(solution)/shard_map/reduce_scatter | solution.py:78
  144.9 10.0 %copy-start.2 = (bf16[8,2,2,768,256]{4,3,0,2,1:T(8,128)(2,1)S(1)}, bf16[8,2,2,768,256]{4,3,0,2,1:T(8,128)(2,1)}, u32[]{:S(2)}) copy-start(bf16[8,2,2,768,256]{4,3,0,2,1:T(8,128)(2,1)} %all-gather.2.cloned.1.call-done) | copy-start | bytes 37748740
  149.7 5.3 %copy-start.10 = (bf16[2,128,2048]{2,1,0:T(8,128)(2,1)S(1)}, bf16[2,128,2048]{2,1,0:T(8,128)(2,1)}, u32[]{:S(2)}) copy-start(bf16[2,128,2048]{2,1,0:T(8,128)(2,1)} %param.13) | copy-start | bytes 3145732
  156.9 0.7 copy-start.8
  157.0 5.2 %copy-start.5 = (bf16[2,768,128]{2,1,0:T(8,128)(2,1)}, bf16[2,768,128]{2,1,0:T(8,128)(2,1)S(1)}, u32[]{:S(2)}) copy-start(bf16[2,768,128]{2,1,0:T(8,128)(2,1)S(1)} %get-tuple-element.31) | copy-start | bytes 1179652
  157.0 7.0 %copy-start.7 = (bf16[2,768,128]{2,1,0:T(8,128)(2,1)}, bf16[2,768,128]{2,1,0:T(8,128)(2,1)S(1)}, u32[]{:S(2)}) copy-start(bf16[2,768,128]{2,1,0:T(8,128)(2,1)S(1)} %get-tuple-element.30) | copy-start | bytes 1179652
  162.1 93.2 %reduce-scatter.5.cloned.1.call-start = ((), (), s32[]{:S(2)}) async-start(), calls=%async_computation.7 | async-start | bytes 7077888 | tf_op jit(solution)/shard_map/reduce_scatter | solution.py:79
  168.4 52.3 %copy-start.14 = (bf16[128,256]{1,0:T(8,128)(2,1)S(1)}, bf16[128,256]{1,0:T(8,128)(2,1)}, u32[]{:S(2)}) copy-start(bf16[128,256]{1,0:T(8,128)(2,1)} %param.8) | copy-start | bytes 196612
  210.5 47.7 %all-to-all-start.1 = ((bf16[2,768,256]{2,0,1:T(2,128)(2,1)}), bf16[2,768,256]{2,0,1:T(2,128)(2,1)S(1)}, u32[]{:S(2)}, u32[]{:S(2)}) async-start(bf16[2,768,256]{2,0,1:T(2,128)(2,1)} %copy.71), calls=%async_computation.2 | async-start | bytes 1572864 | tf_op jit(solution)/shard_map/all_to_all | solution.py:82
  258.2 17.4 %copy-start.3 = (bf16[2,768,256]{2,0,1:T(2,128)(2,1)}, bf16[2,768,256]{2,0,1:T(2,128)(2,1)S(1)}, u32[]{:S(2)}) copy-start(bf16[2,768,256]{2,0,1:T(2,128)(2,1)S(1)} %all-to-all-done.1) | copy-start | bytes 2359300
  258.2 61.5 %all-to-all-start.2 = ((bf16[2,768,256]{2,0,1:T(2,128)(2,1)}), bf16[2,768,256]{2,0,1:T(2,128)(2,1)}, u32[]{:S(2)}, u32[]{:S(2)}) async-start(bf16[2,768,256]{2,0,1:T(2,128)(2,1)} %copy.74), calls=%async_computation.4 | async-start | bytes 1572864 | tf_op jit(solution)/shard_map/all_to_all | solution.py:83
  275.6 6.7 %copy-start.6 = (bf16[2,768,128]{2,1,0:T(8,128)(2,1)S(1)}, bf16[2,768,128]{2,1,0:T(8,128)(2,1)}, u32[]{:S(2)}) copy-start(bf16[2,768,128]{2,1,0:T(8,128)(2,1)} %copy-done.5) | copy-start | bytes 1179652
  282.3 6.8 %copy-start.4 = (bf16[2,768,256]{2,0,1:T(2,128)(2,1)S(1)}, bf16[2,768,256]{2,0,1:T(2,128)(2,1)}, u32[]{:S(2)}) copy-start(bf16[2,768,256]{2,0,1:T(2,128)(2,1)} %copy-done.3) | copy-start | bytes 2359300
  282.3 10.8 %copy-start.13 = (f32[128,256]{1,0:T(8,128)S(1)}, f32[128,256]{1,0:T(8,128)}, u32[]{:S(2)}) copy-start(f32[128,256]{1,0:T(8,128)} %convert_element_type.91) | copy-start | bytes 393220
  289.1 32.0 %copy-start.12 = (pred[1536,128]{1,0:T(8,128)(4,1)S(1)}, pred[1536,128]{1,0:T(8,128)(4,1)}, u32[]{:S(2)}) copy-start(pred[1536,128]{1,0:T(8,128)(4,1)} %copy-done.11) | copy-start | bytes 589828
  289.1 33.0 %copy-start.1 = (bf16[2,2048,128]{2,1,0:T(8,128)(2,1)S(1)}, bf16[2,2048,128]{2,1,0:T(8,128)(2,1)}, u32[]{:S(2)}) copy-start(bf16[2,2048,128]{2,1,0:T(8,128)(2,1)} %param.11) | copy-start | bytes 3145732
Sparse Core Ops, SparseCore 0:
  78.2 66.7 all-gather.1
  162.2 45.4 reduce-scatter.2
  210.3 44.9 reduce-scatter.4
where the time goes:
time: 329 us
  waiting for transfers between devices  140 us (43%)
  blocking collectives  75.4 us (23%)
  matrix products  46.6 us (14%)
  starting transfers between devices  20.5 us (6%)
  local copies, waits for them, and re-layouts  16.7 us (5%)
  other arithmetic  15.5 us (5%)
  between operations  14.1 us (4%)
    all_gather x1, waiting for transfers between devices, local(): gathered = lax.all_gather(routed, 'et', axis=0)  66.7 us
    all_to_all x1, blocking collectives, local(): lax.all_to_all(routed, 'dp', split_axis=1, concat_axis=2, tiled=True)  50.7 us
    reduce_scatter x1, waiting for transfers between devices, local(): lax.psum_scatter(out_part.astype(jnp.bfloat16), 'et', scatter_dimension=2...  39.3 us
    reduce_scatter x1, waiting for transfers between devices, local(): lax.psum_scatter(in_part.astype(jnp.bfloat16), 'et', scatter_dimension=2,...  33.8 us
    psum x1, blocking collectives, local(): grad_gates = lax.psum(gate_part, 'et')  24.7 us
    all_to_all x1, starting transfers between devices, local(): lax.all_to_all(out_sum, 'dp', split_axis=1, concat_axis=0, tiled=True)  10.1 us
    all_to_all x1, starting transfers between devices, local(): lax.all_to_all(in_sum, 'dp', split_axis=1, concat_axis=0, tiled=True)  10.1 us
    reduce_sum x1, other arithmetic, local(): jnp.sum(jnp.where(match, route_gates.T[None, :, :].astype(jnp.float32), 0...  8.15 us
  transfers between devices with their start and end apart: 5, of which 3 were waited for; matrix products, arithmetic and copies ran while one was open for 12% of the time, Pallas kernels for 0%

commit v1 on v0

--- a/solution.py
+++ b/solution.py
@@ -94,7 +94,10 @@
         back_out[slot_index.reshape(-1)].reshape(tok_rows, per_token, width).astype(jnp.float32)
     )
     gate_part = jnp.sum(cotangent.astype(jnp.float32)[:, None, :] * out_rows, axis=2)
-    grad_gates = lax.psum(gate_part, "et")
+    n_dev, grad_gates = (lax.axis_size("et"), gate_part)
+    for far in [1 << k for k in range(n_dev.bit_length() - 1)]:
+        swap = [(i, i ^ far) for i in range(n_dev)]
+        grad_gates = grad_gates + lax.ppermute(grad_gates, "et", swap)
     return (mixed, grad_tokens, grad_gates, grad_gate_w, grad_up_w, grad_down)
 
 

time: 329 us -> 314 us (0.954)
  blocking collectives: 75.4 us -> 50.7 us
  waiting for transfers between devices: 140 us -> 148 us
    psum x1 -> x0, blocking collectives: 24.7 us -> none  [local(): grad_gates = lax.psum(gate_part, 'et')]
    ppermute x0 -> x3, waiting for transfers between devices: none -> 7.2 us  [local(): grad_gates = grad_gates + lax.ppermute(grad_gates, 'et', swap)]
  transfers between devices with their start and end apart: 5 -> 8, of which waited for: 3 -> 5; matrix products, arithmetic and copies ran while one was open for 12% -> 13% of each run, Pallas kernels for 0% -> 0%
where the time goes in v1:
time: 314 us; the launch traced here: 313 us
  waiting for transfers between devices  148 us (47%)
  blocking collectives  50.7 us (16%)
  matrix products  47.7 us (15%)
  starting transfers between devices  21.6 us (7%)
  local copies, waits for them, and re-layouts  15.8 us (5%)
  other arithmetic  15.8 us (5%)
  between operations  14 us (4%)
    all_gather x1, waiting for transfers between devices, local(): gathered = lax.all_gather(routed, 'et', axis=0)  66.7 us
    all_to_all x1, blocking collectives, local(): lax.all_to_all(routed, 'dp', split_axis=1, concat_axis=2, tiled=True)  50.7 us
    reduce_scatter x1, waiting for transfers between devices, local(): lax.psum_scatter(out_part.astype(jnp.bfloat16), 'et', scatter_dimension=2...  39.3 us
    reduce_scatter x1, waiting for transfers between devices, local(): lax.psum_scatter(in_part.astype(jnp.bfloat16), 'et', scatter_dimension=2,...  34.5 us
    all_to_all x1, starting transfers between devices, local(): lax.all_to_all(out_sum, 'dp', split_axis=1, concat_axis=0, tiled=True)  10.1 us
    all_to_all x1, starting transfers between devices, local(): lax.all_to_all(in_sum, 'dp', split_axis=1, concat_axis=0, tiled=True)  10 us
    reduce_sum x1, other arithmetic, local(): jnp.sum(jnp.where(match, route_gates.T[None, :, :].astype(jnp.float32), 0...  8.15 us
    ppermute x3, waiting for transfers between devices, local(): grad_gates = grad_gates + lax.ppermute(grad_gates, 'et', swap)  7.2 us
  transfers between devices with their start and end apart: 8, of which 5 were waited for; matrix products, arithmetic and copies ran while one was open for 13% of the time, Pallas kernels for 0%

profile of v1, /device:TPU:2, one launch (start us, length us, event | category | flops | bytes accessed | tf_op | source)
XLA Modules:
  0.0 313.4 jit_solution(3871958704486898405)
XLA Ops:
  7.2 0.0 copy-start
  7.2 0.0 all-gather.2.cloned.1.call-start
  7.2 0.8 convert_bitcast_fusion
  8.0 0.8 copy.65
  8.8 0.1 eq.28
  8.9 0.6 fusion.12
  9.5 0.1 convert_element_type.78
  9.6 5.6 %fusion = pred[1536,128]{1,0:T(8,128)(4,1)S(1)} fusion(s32[8,128]{1,0:T(8,128)S(1)} %copy.67), kind=kLoop, calls=%fused_computation.6 | loop fusion | flops 2949120 | bytes 200704 | tf_op jit(solution)/shard_map/reduce_or | solution.py:33
  15.2 0.0 copy-start.6
  15.2 8.1 %select_reduce_fusion = bf16[1536,128]{1,0:T(8,128)(2,1)S(1)} fusion(f32[8,128]{1,0:T(8,128)S(1)} %convert_bitcast_fusion, s32[8,128]{1,0:T(8,128)S(1)} %copy.67), kind=kLoop, calls=%fused_computation.4 | loop fusion | flops 4521984 | bytes 401408 | tf_op jit(solution)/shard_map/reduce_sum | solution.py:34
  23.4 1.2 convolution_convert_fusion.1
  24.6 0.0 copy-start.3
  24.6 1.3 convolution_convert_fusion.2
  25.9 0.0 copy-done.6
  25.9 0.1 pad_maximum_fusion
  26.1 50.7 %all_to_all.45 = bf16[2,64,24,256]{3,2,0,1:T(8,128)(2,1)S(1)} all-to-all(bf16[2,64,24,256]{3,2,0,1:T(8,128)(2,1)S(1)} %pad_maximum_fusion), channel_id=1, replica_groups=mesh['dp'=32,'et'=8] {'dp'}, dimensions={1} | all-to-all | bytes 3145728 | tf_op jit(solution)/shard_map/all_to_all | solution.py:42
  76.8 1.2 copy.70
  78.0 0.0 all-gather.2.cloned.1.call-update
  78.0 0.2 reduce-scatter.3.cloned.1.call-start
  78.3 66.7 %all-gather.2.cloned.1.call-done = bf16[8,2,2,768,256]{4,3,0,2,1:T(8,128)(2,1)} async-done(((bf16[1,2,2,768,256]{4,3,0,2,1:T(8,128)(2,1)}), bf16[8,2,2,768,256]{4,3,0,2,1:T(8,128)(2,1)}) %all-gather.2.cloned.1.call-update) | async-done | bytes 12582928 | tf_op jit(solution)/shard_map/all_gather | solution.py:43
  144.9 0.0 copy-done.3
  145.0 4.7 %fusion.9 = f32[2,768,128]{2,1,0:T(8,128)S(1)} fusion(bf16[2,8,256,128]{3,2,1,0:T(8,128)(2,1)S(1)} %bitcast.108, bf16[8,2,2,768,256]{4,3,0,2,1:T(8,128)(2,1)} %all-gather.2.cloned.1.call-done), kind=kOutput, calls=%fused_computation.20 | convolution fusion | flops 805306368 | bytes 8126464 | tf_op jit(solution)/shard_map/jesd,ejdf->esf/dot_general | solution.py:50
  149.7 0.0 copy-done
  149.7 0.0 copy-start.5
  149.7 5.2 %fusion.8 = f32[2,768,128]{2,1,0:T(8,128)S(1)} fusion(bf16[2,8,256,128]{3,2,1,0:T(8,128)(2,1)S(1)} %bitcast.96, bf16[8,2,2,768,256]{4,3,0,2,1:T(8,128)(2,1)} %all-gather.2.cloned.1.call-done), kind=kOutput, calls=%fused_computation.19 | convolution fusion | flops 805306368 | bytes 8126464 | tf_op jit(solution)/shard_map/jesd,ejdf->esf/dot_general | solution.py:49
  154.9 0.0 copy-done.2
  154.9 0.0 copy-done.5
  154.9 2.0 multiply_convert_fusion
  156.9 4.4 %convolution_convert_fusion = bf16[2,768,2048]{2,1,0:T(8,128)(2,1)} fusion(bf16[2,768,128]{2,1,0:T(8,128)(2,1)S(1)} %get-tuple-element.32, bf16[2,128,2048]{2,1,0:T(8,128)(2,1)S(1)} %copy-done.5), kind=kOutput, calls=%fused_computation.9 | convolution fusion | flops 808452096 | bytes 7733248 | tf_op jit(solution)/shard_map/esf,efd->esd/dot_general | solution.py:54
  161.3 0.0 reduce-scatter.3.cloned.1.call-update
  161.4 0.0 reduce-scatter.5.cloned.1.call-start
  161.4 0.0 copy-start.4
  161.4 1.8 fusion.24
  163.2 4.4 %add_convert_fusion = bf16[2,768,2048]{2,1,0:T(8,128)(2,1)} fusion(f32[2,768,2048]{2,1,0:T(8,128)S(1)} %fusion.24, bf16[2,768,128]{2,1,0:T(8,128)(2,1)S(1)} %get-tuple-element.30, bf16[2,2048,128]{2,1,0:T(8,128)(2,1)S(1)} %copy-done.4), kind=kOutput, calls=%fused_computation.1 | convolution fusion | flops 811597824 | bytes 20316160 | tf_op jit(solution)/shard_map/esf,edf->esd/dot_general | solution.py:74
  167.7 0.0 reduce-scatter.5.cloned.1.call-update
  167.7 39.3 %reduce-scatter.3.cloned.1.call-done = bf16[2,768,256]{2,1,0:T(8,128)(2,1)} async-done(((bf16[2,768,2048]{2,1,0:T(8,128)(2,1)}), bf16[2,768,256]{2,1,0:T(8,128)(2,1)}) %reduce-scatter.3.cloned.1.call-update) | async-done | bytes 786448 | tf_op jit(solution)/shard_map/reduce_scatter | solution.py:78
  207.0 2.8 copy.71
  209.8 10.1 %all-to-all-start.1 = ((bf16[2,768,256]{2,0,1:T(2,128)(2,1)}), bf16[2,768,256]{2,0,1:T(2,128)(2,1)S(1)}, u32[]{:S(2)}, u32[]{:S(2)}) async-start(bf16[2,768,256]{2,0,1:T(2,128)(2,1)} %copy.71), calls=%async_computation.2 | async-start | bytes 1572864 | tf_op jit(solution)/shard_map/all_to_all | solution.py:82
  220.0 0.1 mul.64
  220.1 34.5 %reduce-scatter.5.cloned.1.call-done = bf16[2,768,256]{2,1,0:T(8,128)(2,1)} async-done(((bf16[2,768,2048]{2,1,0:T(8,128)(2,1)}), bf16[2,768,256]{2,1,0:T(8,128)(2,1)}) %reduce-scatter.5.cloned.1.call-update) | async-done | bytes 786448 | tf_op jit(solution)/shard_map/reduce_scatter | solution.py:79
  254.6 2.8 copy.74
  257.4 0.0 all-to-all-done.1
  257.4 10.0 %all-to-all-start.2 = ((bf16[2,768,256]{2,0,1:T(2,128)(2,1)}), bf16[2,768,256]{2,0,1:T(2,128)(2,1)S(1)}, u32[]{:S(2)}, u32[]{:S(2)}) async-start(bf16[2,768,256]{2,0,1:T(2,128)(2,1)} %copy.74), calls=%async_computation.4 | async-start | bytes 1572864 | tf_op jit(solution)/shard_map/all_to_all | solution.py:83
  267.5 6.7 %fusion.4 = f32[2,8,256,128]{3,2,1,0:T(8,128)} fusion(bf16[8,2,2,768,256]{4,3,0,2,1:T(8,128)(2,1)} %all-gather.2.cloned.1.call-done, bf16[2,768,128]{2,1,0:T(8,128)(2,1)S(1)} %get-tuple-element.30), kind=kOutput, calls=%fused_computation.12 | convolution fusion | flops 805306368 | bytes 8781824 | tf_op jit(solution)/shard_map/jesd,esf->ejdf/dot_general | solution.py:68
  274.1 6.7 %fusion.5 = f32[2,8,256,128]{3,2,1,0:T(8,128)} fusion(bf16[8,2,2,768,256]{4,3,0,2,1:T(8,128)(2,1)} %all-gather.2.cloned.1.call-done, bf16[2,768,128]{2,1,0:T(8,128)(2,1)S(1)} %get-tuple-element.31), kind=kOutput, calls=%fused_computation.13 | convolution fusion | flops 805306368 | bytes 8781824 | tf_op jit(solution)/shard_map/jesd,esf->ejdf/dot_general | solution.py:65
  280.8 0.1 copy.72
  280.9 3.9 %gather_fusion = bf16[1024,256]{1,0:T(8,128)(2,1)S(1)} fusion(bf16[1536,256]{1,0:T(8,128)(2,1)S(1)} %bitcast.97, s32[1024]{0:T(1024)S(1)} %broadcast_clamp_fusion), kind=kCustom, calls=%fused_computation | custom fusion | bytes 1052672 | tf_op jit(solution)/shard_map/gather | solution.py:94
  284.9 0.2 fusion.15
  285.1 0.1 collective-permute-start
  285.2 0.0 copy-start.1
  285.2 6.8 %fusion.1 = f32[2,128,8,256]{1,3,2,0:T(8,128)} fusion(bf16[8,2,2,768,256]{4,3,0,2,1:T(8,128)(2,1)} %all-gather.2.cloned.1.call-done, bf16[2,768,128]{2,1,0:T(8,128)(2,1)S(1)} %get-tuple-element.32), kind=kOutput, calls=%fused_computation.7 | convolution fusion | flops 805306368 | bytes 8781824 | tf_op jit(solution)/shard_map/esf,jesd->efjd/dot_general | solution.py:62
  292.0 2.9 copy.82
  294.9 0.0 collective-permute-done
  294.9 0.8 add.55
  295.7 0.1 collective-permute-start.1
  295.8 1.0 convolution_convert_fusion.3
  296.8 0.0 all-to-all-done.2
  296.8 0.1 copy.75
  296.9 0.1 copy.76
  297.0 3.3 %collective-permute-done.1 = f32[128,8]{1,0:T(8,128)S(1)} collective-permute-done((f32[128,8]{1,0:T(8,128)S(1)}, f32[128,8]{1,0:T(8,128)S(1)}, u32[]{:S(2)}, u32[]{:S(2)}) %collective-permute-start.1) | collective-permute-done | bytes 4128 | tf_op jit(solution)/shard_map/ppermute | solution.py:100
  300.3 0.9 collective-permute-start.2
  301.2 1.1 convolution_convert_fusion.4
  302.3 3.9 %collective-permute-done.2 = f32[128,8]{1,0:T(8,128)S(1)} collective-permute-done((f32[128,8]{1,0:T(8,128)S(1)}, f32[128,8]{1,0:T(8,128)S(1)}, u32[]{:S(2)}, u32[]{:S(2)}) %collective-permute-start.2) | collective-permute-done | bytes 4128 | tf_op jit(solution)/shard_map/ppermute | solution.py:100
  306.2 0.7 copy.81
  (15 shorter events, 0.1 us)
Async XLA Ops:
  7.2 142.5 %copy-start = (bf16[2,2048,128]{2,1,0:T(8,128)(2,1)S(1)}, bf16[2,2048,128]{2,1,0:T(8,128)(2,1)}, u32[]{:S(2)}) copy-start(bf16[2,2048,128]{2,1,0:T(8,128)(2,1)} %param.11) | copy-start | bytes 3145732
  7.2 137.8 %all-gather.2.cloned.1.call-start = ((), (), s32[]{:S(2)}) async-start(), calls=%async_computation.5 | async-start | bytes 14155776 | tf_op jit(solution)/shard_map/all_gather | solution.py:43
  15.2 10.7 %copy-start.6 = (pred[1536,128]{1,0:T(8,128)(4,1)}, pred[1536,128]{1,0:T(8,128)(4,1)S(1)}, u32[]{:S(2)}) copy-start(pred[1536,128]{1,0:T(8,128)(4,1)S(1)} %fusion) | copy-start | bytes 589828
  24.6 120.4 %copy-start.3 = (bf16[2,2048,128]{2,1,0:T(8,128)(2,1)S(1)}, bf16[2,2048,128]{2,1,0:T(8,128)(2,1)}, u32[]{:S(2)}) copy-start(bf16[2,2048,128]{2,1,0:T(8,128)(2,1)} %param.12) | copy-start | bytes 3145732
  78.0 128.9 %reduce-scatter.3.cloned.1.call-start = ((), (), s32[]{:S(2)}) async-start(), calls=%async_computation.6 | async-start | bytes 7077888 | tf_op jit(solution)/shard_map/reduce_scatter | solution.py:78
  144.9 10.0 %copy-start.2 = (bf16[8,2,2,768,256]{4,3,0,2,1:T(8,128)(2,1)S(1)}, bf16[8,2,2,768,256]{4,3,0,2,1:T(8,128)(2,1)}, u32[]{:S(2)}) copy-start(bf16[8,2,2,768,256]{4,3,0,2,1:T(8,128)(2,1)} %all-gather.2.cloned.1.call-done) | copy-start | bytes 37748740
  149.7 5.3 %copy-start.5 = (bf16[2,128,2048]{2,1,0:T(8,128)(2,1)S(1)}, bf16[2,128,2048]{2,1,0:T(8,128)(2,1)}, u32[]{:S(2)}) copy-start(bf16[2,128,2048]{2,1,0:T(8,128)(2,1)} %param.13) | copy-start | bytes 3145732
  161.4 93.3 %reduce-scatter.5.cloned.1.call-start = ((), (), s32[]{:S(2)}) async-start(), calls=%async_computation.7 | async-start | bytes 7077888 | tf_op jit(solution)/shard_map/reduce_scatter | solution.py:79
  161.4 1.8 copy-start.4
  167.7 52.3 %copy-start.8 = (bf16[128,256]{1,0:T(8,128)(2,1)S(1)}, bf16[128,256]{1,0:T(8,128)(2,1)}, u32[]{:S(2)}) copy-start(bf16[128,256]{1,0:T(8,128)(2,1)} %param.8) | copy-start | bytes 196612
  209.8 47.6 %all-to-all-start.1 = ((bf16[2,768,256]{2,0,1:T(2,128)(2,1)}), bf16[2,768,256]{2,0,1:T(2,128)(2,1)S(1)}, u32[]{:S(2)}, u32[]{:S(2)}) async-start(bf16[2,768,256]{2,0,1:T(2,128)(2,1)} %copy.71), calls=%async_computation.2 | async-start | bytes 1572864 | tf_op jit(solution)/shard_map/all_to_all | solution.py:82
  257.4 39.4 %all-to-all-start.2 = ((bf16[2,768,256]{2,0,1:T(2,128)(2,1)}), bf16[2,768,256]{2,0,1:T(2,128)(2,1)S(1)}, u32[]{:S(2)}, u32[]{:S(2)}) async-start(bf16[2,768,256]{2,0,1:T(2,128)(2,1)} %copy.74), calls=%async_computation.4 | async-start | bytes 1572864 | tf_op jit(solution)/shard_map/all_to_all | solution.py:83
  285.1 9.8 %collective-permute-start = (f32[128,8]{1,0:T(8,128)S(1)}, f32[128,8]{1,0:T(8,128)}, u32[]{:S(2)}, u32[]{:S(2)}) collective-permute-start(f32[128,8]{1,0:T(8,128)S(1)} %fusion.15), channel_id=1, source_target_pairs={{0,1},{1,0},{2,3},{3,2},{4,5},{5,4},{6,7},{7,6},{8,9},{9,8},{10,11... | collective-permute-start | bytes 12296 | tf_op jit(solution)/shard_map/ppermute | solution.py:100
  285.2 21.7 %copy-start.1 = (bf16[2,2048,128]{2,1,0:T(8,128)(2,1)S(1)}, bf16[2,2048,128]{2,1,0:T(8,128)(2,1)}, u32[]{:S(2)}) copy-start(bf16[2,2048,128]{2,1,0:T(8,128)(2,1)} %param.11) | copy-start | bytes 3145732
  292.0 9.3 %copy-start.7 = (pred[1536,128]{1,0:T(8,128)(4,1)S(1)}, pred[1536,128]{1,0:T(8,128)(4,1)}, u32[]{:S(2)}) copy-start(pred[1536,128]{1,0:T(8,128)(4,1)} %copy-done.6) | copy-start | bytes 589828
  295.7 4.6 %collective-permute-start.1 = (f32[128,8]{1,0:T(8,128)S(1)}, f32[128,8]{1,0:T(8,128)S(1)}, u32[]{:S(2)}, u32[]{:S(2)}) collective-permute-start(f32[128,8]{1,0:T(8,128)S(1)} %add.55), channel_id=1, source_target_pairs={{0,2},{1,3},{2,0},{3,1},{4,6},{5,7},{6,4},{7,5},{8,10},{9,11},{10,... | collective-permute-start | bytes 12296 | tf_op jit(solution)/shard_map/ppermute | solution.py:100
  300.3 5.9 %collective-permute-start.2 = (f32[128,8]{1,0:T(8,128)S(1)}, f32[128,8]{1,0:T(8,128)S(1)}, u32[]{:S(2)}, u32[]{:S(2)}) collective-permute-start(f32[128,8]{1,0:T(8,128)S(1)} %add.56), channel_id=1, source_target_pairs={{0,4},{1,5},{2,6},{3,7},{4,0},{5,1},{6,2},{7,3},{8,12},{9,13},{10,... | collective-permute-start | bytes 12296 | tf_op jit(solution)/shard_map/ppermute | solution.py:100
Sparse Core Ops, SparseCore 0:
  78.2 66.7 all-gather.1
  161.5 45.4 reduce-scatter.2
  209.5 45.0 reduce-scatter.4
